TPU v7x, 32 devices: a whole 2x2x4 slice. The times are simulated.
32 devices in a mesh: tm: 4 (over z), space: 2 (over y), hyp: 4 (over x, core).
Axes of the slice: x: 2, y: 2, z: 4, core: 2. Of those that a mesh axis runs over, the one named last changes fastest.
Arguments:
- log_kappa: float32 [8192], P('space'), may hold values from -0.5 to 0.5
- node_mass: float32 [8192], P('space'), may hold values from 0.5 to 2
- rho_base: float32 [8192], P('space'), may hold values from 1.5 to 4
- edge_weight: float32 [4, 8192], P(None, 'space'), may hold values from 0.05 to 0.3
- offsets: int32 [4, 8192], P(None, 'space'), may hold values from -64 to 64
- roughness: float32 [64, 8192], P('tm', 'space'), may hold values from 0.5 to 1.0002
- coupling: float32 [64, 8192], P('tm', 'space'), may hold values from 0.5 to 1
- obs_weight: float32 [64, 8192], P('tm', 'space'), may hold values from 0.0003 to 0.03
- observed: float32 [64, 8192], P('tm', 'space'), may hold values from -0.3125 to 0.3125
- hyper_params: float32 [4], replicated, may hold values from -0.3 to 0.3
Outputs:
- solution: float32 [64, 8192], P('tm', ('space', 'hyp'))
- log_det_mean: float32 [8192], P('space')
- gradient: float32 [4, 8192], P(None, 'space')
Inputs may be any that keep to these rules, and one draw needn't show every extreme that they name: offsets[k, i] is a band offset from node i to a listed neighbour.
All inputs are finite; a program needn't handle non-finite values.
Results may differ from a plain program's by a relative error of at most 0.0003.
Values sent between devices are 32-bit elements; how exact they have to be, the bound alone decides.
No kernel may reach another device: no remote copies, remote signals or barrier semaphores. Data moves between devices by JAX's collectives and lax.ppermute only.
A program may use at most 64 MiB of HBM per device.

v0:
```python
import jax
import jax.numpy as jnp
from jax import lax
from jax.sharding import PartitionSpec as P

BAND = 64


def with_halo(block, sides, width):
    for axis, dim in sides:
        count = lax.axis_size(axis)
        forward = [(i, i + 1) for i in range(count - 1)]
        backward = [(target, source) for source, target in forward]
        low = lax.ppermute(
            lax.slice_in_dim(block, block.shape[dim] - width, None, axis=dim), axis, forward
        )
        high = lax.ppermute(lax.slice_in_dim(block, 0, width, axis=dim), axis, backward)
        block = jnp.concatenate([low, block, high], axis=dim)
    return block


def prefix(part, axis, combine, identity, reverse):
    count = lax.axis_size(axis)
    place = lax.axis_index(axis)
    ahead = count - 1 - place if reverse else place
    gathered = jax.tree.map(lambda a: lax.all_gather(a, axis), part)
    state = jax.tree.map(lambda a, e: jnp.zeros_like(a) + jnp.asarray(e, a.dtype), part, identity)

    def one(hop, state):
        source = count - 1 - hop if reverse else hop
        return combine(
            state, jax.tree.map(lambda a: lax.dynamic_index_in_dim(a, source, 0, False), gathered)
        )

    return lax.fori_loop(0, ahead, one, state)


def row_terms(scaled, persist, roughness, coupling, obs_weight, nugget_scale, later_rows):
    prior = scaled * (1.0 + persist * persist) * roughness
    nugget = nugget_scale * obs_weight
    diagonal = prior + nugget
    offdiag = -persist * scaled * coupling * later_rows
    slopes = jnp.stack(
        [
            2.0 * prior,
            prior,
            2.0 * persist * (1.0 - persist * persist) * scaled * roughness,
            nugget,
        ],
        axis=-2,
    )
    return (diagonal, offdiag, slopes)


def mobius_join(earlier_part, later_part):
    upper_left = later_part[0] * earlier_part[0] + later_part[1] * earlier_part[2]
    upper_right = later_part[0] * earlier_part[1] + later_part[1] * earlier_part[3]
    lower_left = later_part[2] * earlier_part[0] + later_part[3] * earlier_part[2]
    lower_right = later_part[2] * earlier_part[1] + later_part[3] * earlier_part[3]
    norm_total = (
        jnp.abs(upper_left) + jnp.abs(upper_right) + jnp.abs(lower_left) + jnp.abs(lower_right)
    )
    return (
        upper_left / norm_total,
        upper_right / norm_total,
        lower_left / norm_total,
        lower_right / norm_total,
    )


def affine_join(earlier_part, later_part):
    joined = []
    for index in range(0, len(earlier_part), 2):
        joined.append(later_part[index] * earlier_part[index])
        joined.append(later_part[index] * earlier_part[index + 1] + later_part[index + 1])
    return tuple(joined)


def mobius_step(carried, step_rows):
    diag_row, off_row = step_rows
    step_map = (diag_row, -off_row * off_row, jnp.ones_like(diag_row), jnp.zeros_like(diag_row))
    return (mobius_join(carried, step_map), None)


def per_device(
    log_kappa,
    node_mass,
    rho_base,
    edge_weight,
    offsets,
    roughness,
    coupling,
    obs_weight,
    observed,
    hyper_params,
):
    row_count, full_width = roughness.shape
    kappa_sq = jnp.exp(2.0 * log_kappa)
    padded = with_halo(kappa_sq, (("space", 0),), BAND)
    indices = jnp.arange(full_width, dtype=jnp.int32)[None, :] + BAND + offsets
    nearby = jnp.take(padded, indices)
    spatial = jnp.exp(2.0 * hyper_params[0]) * (
        node_mass * kappa_sq + jnp.sum(edge_weight * nearby, axis=0)
    )
    scaled = jnp.exp(hyper_params[1]) * spatial
    persist = jnp.tanh(hyper_params[2] + rho_base)
    nugget_scale = jnp.exp(hyper_params[3])
    log_slope = jnp.stack(
        [
            2.0 * jnp.ones_like(persist),
            jnp.ones_like(persist),
            (1.0 - persist * persist) / persist,
            jnp.zeros_like(persist),
        ]
    )
    hyp_count = lax.axis_size("hyp")
    hyp_place = lax.axis_index("hyp")
    quarter = full_width // hyp_count
    time_count = lax.axis_size("tm")
    global_rows = jnp.arange(row_count, dtype=jnp.int32) + lax.axis_index("tm") * row_count
    later_rows = (global_rows > 0).astype(jnp.float32)[:, None]
    diagonal, offdiag, slopes = row_terms(
        scaled, persist, roughness, coupling, obs_weight, nugget_scale, later_rows
    )
    slopes = lax.dynamic_index_in_dim(slopes, hyp_place, 1, keepdims=True)
    log_slope = lax.dynamic_index_in_dim(log_slope, hyp_place, 0, keepdims=True)
    ones_row = jnp.ones_like(diagonal[0])
    zeros_row = jnp.zeros_like(diagonal[0])
    zeros_dir = jnp.zeros_like(log_slope)
    identity = (ones_row, zeros_row, zeros_row, ones_row)
    local_map, unused = lax.scan(mobius_step, identity, (diagonal, offdiag))
    before = prefix(local_map, "tm", mobius_join, identity, False)
    inverse_in = before[2] / before[0]

    def forward_step(carried, step_rows):
        inverse, gain_tangent, tangent_loc, gain_solve, solve_loc = carried
        diag_row, off_row, slope_row, observed_row = step_rows
        pivots = diag_row - off_row * off_row * inverse
        ratios = off_row * inverse
        gain_tangent = ratios * ratios * gain_tangent
        tangent_loc = ratios * ratios * tangent_loc + slope_row - 2.0 * log_slope * off_row * ratios
        gain_solve = -ratios * gain_solve
        solve_loc = observed_row - ratios * solve_loc
        return (
            (1.0 / pivots, gain_tangent, tangent_loc, gain_solve, solve_loc),
            (pivots, gain_tangent, tangent_loc, gain_solve, solve_loc),
        )

    start = (inverse_in, ones_row, zeros_dir, ones_row, zeros_row)
    ending, stacked = lax.scan(forward_step, start, (diagonal, offdiag, slopes, observed))
    pivots, gains_tangent, tangent_locs, gains_solve, solve_locs = stacked
    incoming = prefix(
        (ending[1], ending[2], ending[3], ending[4]),
        "tm",
        affine_join,
        (ones_row, zeros_dir, ones_row, zeros_row),
        False,
    )
    tangents = tangent_locs + gains_tangent[:, None, :] * incoming[1][None]
    solveds = solve_locs + gains_solve * incoming[3][None]

    def backward_step(carried, step_rows):
        next_loc, next_gain = carried
        off_row, pivot_row, solved_row = step_rows
        return (
            (off_row * (solved_row - next_loc) / pivot_row, -off_row / pivot_row * next_gain),
            (next_loc, next_gain),
        )

    front, trailing = lax.scan(
        backward_step, (zeros_row, ones_row), (offdiag, pivots, solveds), reverse=True
    )
    next_locs, next_gains = trailing
    after = prefix((front[1], front[0]), "tm", affine_join, (ones_row, zeros_row), True)
    carried_next = next_locs + next_gains * after[1][None]
    solution = (solveds - carried_next) / pivots
    total_rows = row_count * time_count
    scores = jnp.sum(0.5 * tangents / pivots[:, None, :], axis=0)
    quadratic = jnp.sum(
        slopes * (solution * solution)[:, None, :]
        + 2.0 * log_slope[None] * (solution * carried_next)[:, None, :],
        axis=0,
    )
    gradient_part = (scores - 0.5 * quadratic) / total_rows
    logdet_part = jnp.sum(jnp.log(pivots), axis=0) / total_rows
    direction_mask = (jnp.arange(hyp_count, dtype=jnp.int32) == hyp_place).astype(jnp.float32)[
        :, None
    ]
    leader_mask = (hyp_place == 0).astype(jnp.float32)
    placed = jnp.concatenate(
        [(leader_mask * logdet_part)[None], direction_mask * gradient_part], axis=0
    )
    solution_out = lax.dynamic_slice_in_dim(
        solution, hyp_place * quarter, quarter, solution.ndim - 1
    )
    totals = lax.psum(placed, ("tm", "hyp"))
    return (solution_out, totals[0], totals[1:])


def solution(mesh):
    placed = (
        P("space"),
        P("space"),
        P("space"),
        P(None, "space"),
        P(None, "space"),
        P("tm", "space"),
        P("tm", "space"),
        P("tm", "space"),
        P("tm", "space"),
        P(),
    )
    return jax.shard_map(
        per_device,
        mesh=mesh,
        in_specs=placed,
        out_specs=(P("tm", ("space", "hyp")), P("space"), P(None, "space")),
        check_vma=False,
    )
```

profile of v0, /device:TPU:8, one launch (start us, length us, event | category | flops | bytes accessed | tf_op | source)
XLA Modules:
  0.0 407.8 jit_solution(9264937598001699120)
XLA Ops:
  8.0 3.4 collective-permute-start
  11.4 1.3 collective-permute-start.1
  17.1 90.5 %gather_fusion = f32[16384]{0:T(1024)S(1)} fusion(f32[4224]{0:T(1024)S(1)} %concatenate.6, s32[16384]{0:T(1024)S(1)} %broadcast_clamp_fusion), kind=kCustom, calls=%fused_computation | custom fusion | bytes 196608 | tf_op jit(solution)/shard_map/jit(_take)/gather | solution.py:101
  109.3 2.1 while.116
  111.4 13.4 %all-gather = f32[16384]{0:T(1024)S(1)} all-gather(f32[4096]{0:T(1024)S(1)} %get-tuple-element.526), channel_id=2, replica_groups=mesh['tm'=4,'space'=2,'hyp'=4] {'tm'}, dimensions={0}, use_global_device_ids=true | all-gather | bytes 81920 | tf_op jit(solution)/shard_map/all_gather | solution.py:26
  124.8 13.2 %all-gather.1 = f32[16384]{0:T(1024)S(1)} all-gather(f32[4096]{0:T(1024)S(1)} %get-tuple-element.527), channel_id=3, replica_groups=mesh['tm'=4,'space'=2,'hyp'=4] {'tm'}, dimensions={0}, use_global_device_ids=true | all-gather | bytes 81920 | tf_op jit(solution)/shard_map/all_gather | solution.py:26
  138.0 13.1 %all-gather.2 = f32[16384]{0:T(1024)S(1)} all-gather(f32[4096]{0:T(1024)S(1)} %get-tuple-element.528), channel_id=4, replica_groups=mesh['tm'=4,'space'=2,'hyp'=4] {'tm'}, dimensions={0}, use_global_device_ids=true | all-gather | bytes 81920 | tf_op jit(solution)/shard_map/all_gather | solution.py:26
  151.1 13.1 %all-gather.3 = f32[16384]{0:T(1024)S(1)} all-gather(f32[4096]{0:T(1024)S(1)} %get-tuple-element.529), channel_id=5, replica_groups=mesh['tm'=4,'space'=2,'hyp'=4] {'tm'}, dimensions={0}, use_global_device_ids=true | all-gather | bytes 81920 | tf_op jit(solution)/shard_map/all_gather | solution.py:26
  165.5 43.2 %while.117 = (s32[]{:T(128)}, f32[4096]{0:T(1024)S(1)}, f32[4096]{0:T(1024)S(1)}, f32[1,4096]{1,0:T(1,128)S(1)}, f32[4096]{0:T(1024)S(1)}, /*index=5*/f32[4096]{...) while((s32[]{:T(128)}, f32[4096]{0:T(1024)S(1)}, ...), condition=%wide.region_6.7_spmd.clone, body=%wide.region_5.6_spmd.clone.sunk | while | flops 86019 | bytes 606413 | solution.py:150
  165.5 0.9 constant_dynamic-slice_fusion.31
  170.9 0.9 constant_dynamic-slice_fusion.31
  184.4 0.9 constant_dynamic-slice_fusion.31
  189.8 0.9 constant_dynamic-slice_fusion.31
  203.3 0.9 constant_dynamic-slice_fusion.31
  208.7 13.5 %all-gather.4 = f32[16384]{0:T(1024)S(1)} all-gather(f32[4096]{0:T(1024)S(1)} %get-tuple-element.534), channel_id=6, replica_groups=mesh['tm'=4,'space'=2,'hyp'=4] {'tm'}, dimensions={0}, use_global_device_ids=true | all-gather | bytes 81920 | tf_op jit(solution)/shard_map/all_gather | solution.py:26
  222.3 13.3 %all-gather.6 = f32[16384]{0:T(1024)S(1)} all-gather(f32[4096]{0:T(1024)S(1)} %get-tuple-element.536), channel_id=8, replica_groups=mesh['tm'=4,'space'=2,'hyp'=4] {'tm'}, dimensions={0}, use_global_device_ids=true | all-gather | bytes 81920 | tf_op jit(solution)/shard_map/all_gather | solution.py:26
  235.6 13.1 %all-gather.7 = f32[16384]{0:T(1024)S(1)} all-gather(f32[4096]{0:T(1024)S(1)} %get-tuple-element.537), channel_id=9, replica_groups=mesh['tm'=4,'space'=2,'hyp'=4] {'tm'}, dimensions={0}, use_global_device_ids=true | all-gather | bytes 81920 | tf_op jit(solution)/shard_map/all_gather | solution.py:26
  248.8 13.1 %all-gather.10 = f32[4,1,4096]{2,1,0:T(1,128)S(1)} all-gather(f32[1,1,4096]{2,1,0:T(1,128)S(1)} %bitcast.142), channel_id=7, replica_groups=mesh['tm'=4,'space'=2,'hyp'=4] {'tm'}, dimensions={0}, use_global_device_ids=true | all-gather | bytes 81920 | tf_op jit(solution)/shard_map/all_gather | solution.py:26
  262.2 14.6 %while.118 = (s32[]{:T(128)}, f32[4096]{0:T(1024)S(1)}, f32[4096]{0:T(1024)S(1)}, f32[16,4096]{1,0:T(8,128)S(1)}, f32[16,4096]{1,0:T(8,128)S(1)}, /*index=5*/f32...) while((s32[]{:T(128)}, f32[4096]{0:T(1024)S(1)}, ...), condition=%wide.region_10.11_spmd.clone, body=%wide.region_9.10_spmd.clone.sunk | while | flops 32772 | bytes 311443 | solution.py:170
  276.8 13.4 %all-gather.8 = f32[16384]{0:T(1024)S(1)} all-gather(f32[4096]{0:T(1024)S(1)} %get-tuple-element.542), channel_id=10, replica_groups=mesh['tm'=4,'space'=2,'hyp'=4] {'tm'}, dimensions={0}, use_global_device_ids=true | all-gather | bytes 81920 | tf_op jit(solution)/shard_map/all_gather | solution.py:26
  290.2 13.1 %all-gather.9 = f32[16384]{0:T(1024)S(1)} all-gather(f32[4096]{0:T(1024)S(1)} %get-tuple-element.543), channel_id=11, replica_groups=mesh['tm'=4,'space'=2,'hyp'=4] {'tm'}, dimensions={0}, use_global_device_ids=true | all-gather | bytes 81920 | tf_op jit(solution)/shard_map/all_gather | solution.py:26
  305.7 92.2 %all-reduce.2.cloned.1.call-done = f32[5,4096]{1,0:T(8,128)} async-done(((f32[5,4096]{1,0:T(8,128)}), f32[5,4096]{1,0:T(8,128)}) %all-reduce.2.cloned.1.call-update) | async-done | bytes 81936 | tf_op jit(solution)/shard_map/psum | solution.py:196
  397.9 1.6 slice.37
  399.4 1.5 slice.36
  (383 shorter events, 60.8 us)
Async XLA Ops:
  7.2 5.7 %copy-start.3 = (s32[4,4096]{1,0:T(4,128)S(1)}, s32[4,4096]{1,0:T(4,128)}, u32[]{:S(2)}) copy-start(s32[4,4096]{1,0:T(4,128)} %param.26) | copy-start | bytes 196612
  7.2 390.7 %all-reduce.2.cloned.1.call-start = ((), (), s32[]{:S(2)}) async-start(), calls=%async_computation | async-start | bytes 262144 | tf_op jit(solution)/shard_map/psum | solution.py:196
  8.0 8.9 %collective-permute-start = (f32[64]{0:T(128)S(1)}, f32[64]{0:T(128)S(1)}, u32[]{:S(2)}, u32[]{:S(2)}) collective-permute-start(f32[64]{0:T(128)S(1)} %get-tuple-element.865), channel_id=1, source_target_pairs={{0,4},{1,5},{2,6},{3,7},{8,12},{9,13},{10,14},{11,15},{16,20},{17,... | collective-permute-start | bytes 776 | tf_op jit(solution)/shard_map/ppermute | solution.py:14
  11.4 5.5 %collective-permute-start.1 = (f32[64]{0:T(128)S(1)}, f32[64]{0:T(128)S(1)}, u32[]{:S(2)}, u32[]{:S(2)}) collective-permute-start(f32[64]{0:T(128)S(1)} %get-tuple-element.864), channel_id=1, source_target_pairs={{4,0},{5,1},{6,2},{7,3},{12,8},{13,9},{14,10},{15,11},{20,16},{21,... | collective-permute-start | bytes 776 | tf_op jit(solution)/shard_map/ppermute | solution.py:17
  12.9 0.7 copy-start.8
  17.1 90.7 %copy-start.4 = (f32[4,4096]{1,0:T(4,128)S(1)}, f32[4,4096]{1,0:T(4,128)}, u32[]{:S(2)}) copy-start(f32[4,4096]{1,0:T(4,128)} %param.25) | copy-start | bytes 196612
  17.1 90.8 %copy-start.5 = (f32[4096]{0:T(1024)S(1)}, f32[4096]{0:T(1024)}, u32[]{:S(2)}) copy-start(f32[4096]{0:T(1024)} %param.24) | copy-start | bytes 49156
  17.1 90.7 %copy-start.6 = (f32[4096]{0:T(1024)S(1)}, f32[4096]{0:T(1024)}, u32[]{:S(2)}) copy-start(f32[4096]{0:T(1024)} %param.22) | copy-start | bytes 49156
  17.1 90.7 %copy-start.7 = (f32[4096]{0:T(1024)S(1)}, f32[4096]{0:T(1024)}, u32[]{:S(2)}) copy-start(f32[4096]{0:T(1024)} %param.23) | copy-start | bytes 49156
  17.1 92.1 %copy-start.2 = (f32[16,4096]{1,0:T(8,128)S(1)}, f32[16,4096]{1,0:T(8,128)}, u32[]{:S(2)}) copy-start(f32[16,4096]{1,0:T(8,128)} %param.28) | copy-start | bytes 786436
  107.7 1.5 copy-start
  107.7 1.5 copy-start.1
Sparse Core Ops, SparseCore 0:
  305.2 92.6 all-reduce.1
where the time goes:
time: 408 us
  local copies, waits for them, and re-layouts  151 us (37%)
  blocking collectives  132 us (32%)
  waiting for transfers between devices  92.2 us (23%)
  between operations  16.7 us (4%)
  other arithmetic  7.32 us (2%)
  starting transfers between devices  4.74 us (1%)
    all_gather x10, blocking collectives, prefix(): gathered = jax.tree.map(lambda a: lax.all_gather(a, axis), part)  132 us
    psum x1, waiting for transfers between devices, per_device(): totals = lax.psum(placed, ('tm', 'hyp'))  92.2 us
    gather x2, local copies, waits for them, and re-layouts, per_device(): nearby = jnp.take(padded, indices)  90.6 us
    dynamic_update_slice x96, local copies, waits for them, and re-layouts, per_device(): lax.scan(forward_step, start, (diagonal, offdiag, slopes, observed))  37.7 us
    dynamic_slice x80, local copies, waits for them, and re-layouts, per_device(): local_map, unused = lax.scan(mobius_step, identity, (diagonal, offdiag))  16.6 us
  transfers between devices with their start and end apart: 3, of which 1 were waited for; matrix products, arithmetic and copies ran while one was open for 0% of the time, Pallas kernels for 0%

commit v1 on v0

--- a/solution.py
+++ b/solution.py
@@ -193,7 +193,7 @@
     solution_out = lax.dynamic_slice_in_dim(
         solution, hyp_place * quarter, quarter, solution.ndim - 1
     )
-    totals = lax.psum(placed, ("tm", "hyp"))
+    totals = jnp.sum(lax.all_gather(placed, ("tm", "hyp")), axis=0)
     return (solution_out, totals[0], totals[1:])
 
 

time: 408 us -> 362 us (0.89)
  waiting for transfers between devices: 92.2 us -> 41.7 us
    psum x1 -> x0, waiting for transfers between devices: 92.2 us -> none  [per_device(): totals = lax.psum(placed, ('tm', 'hyp'))]
    all_gather x0 -> x1, waiting for transfers between devices: none -> 41.7 us  [per_device(): totals = jnp.sum(lax.all_gather(placed, ('tm', 'hyp')), axis=0)]
  transfers between devices with their start and end apart: 3 -> 3, of which waited for: 1 -> 1; matrix products, arithmetic and copies ran while one was open for 0% -> 1% of each run, Pallas kernels for 0% -> 0%
where the time goes in v1:
time: 362 us; the launch traced here: 358 us
  local copies, waits for them, and re-layouts  150 us (41%)
  blocking collectives  132 us (36%)
  waiting for transfers between devices  41.7 us (12%)
  between operations  16.8 us (5%)
  other arithmetic  9.9 us (3%)
  starting transfers between devices  4.74 us (1%)
    all_gather x10, blocking collectives, prefix(): gathered = jax.tree.map(lambda a: lax.all_gather(a, axis), part)  132 us
    gather x2, local copies, waits for them, and re-layouts, per_device(): nearby = jnp.take(padded, indices)  90.6 us
    all_gather x1, waiting for transfers between devices, per_device(): totals = jnp.sum(lax.all_gather(placed, ('tm', 'hyp')), axis=0)  41.7 us
    dynamic_update_slice x96, local copies, waits for them, and re-layouts, per_device(): lax.scan(forward_step, start, (diagonal, offdiag, slopes, observed))  37.6 us
    dynamic_slice x80, local copies, waits for them, and re-layouts, per_device(): local_map, unused = lax.scan(mobius_step, identity, (diagonal, offdiag))  16.6 us
  transfers between devices with their start and end apart: 3, of which 1 were waited for; matrix products, arithmetic and copies ran while one was open for 1% of the time, Pallas kernels for 0%

profile of v1, /device:TPU:8, one launch (start us, length us, event | category | flops | bytes accessed | tf_op | source)
XLA Modules:
  0.0 358.4 jit_solution(13477426227941864380)
XLA Ops:
  8.0 3.4 collective-permute-start
  11.4 1.3 collective-permute-start.1
  13.8 1.5 fusion.22
  18.3 90.5 %gather_fusion = f32[16384]{0:T(1024)S(1)} fusion(f32[4224]{0:T(1024)S(1)} %concatenate.6, s32[16384]{0:T(1024)S(1)} %broadcast_clamp_fusion), kind=kCustom, calls=%fused_computation | custom fusion | bytes 196608 | tf_op jit(solution)/shard_map/jit(_take)/gather | solution.py:101
  110.4 2.1 while.116
  112.5 13.4 %all-gather = f32[16384]{0:T(1024)S(1)} all-gather(f32[4096]{0:T(1024)S(1)} %get-tuple-element.526), channel_id=2, replica_groups=mesh['tm'=4,'space'=2,'hyp'=4] {'tm'}, dimensions={0}, use_global_device_ids=true | all-gather | bytes 81920 | tf_op jit(solution)/shard_map/all_gather | solution.py:26
  125.9 13.2 %all-gather.1 = f32[16384]{0:T(1024)S(1)} all-gather(f32[4096]{0:T(1024)S(1)} %get-tuple-element.527), channel_id=3, replica_groups=mesh['tm'=4,'space'=2,'hyp'=4] {'tm'}, dimensions={0}, use_global_device_ids=true | all-gather | bytes 81920 | tf_op jit(solution)/shard_map/all_gather | solution.py:26
  139.0 13.1 %all-gather.2 = f32[16384]{0:T(1024)S(1)} all-gather(f32[4096]{0:T(1024)S(1)} %get-tuple-element.528), channel_id=4, replica_groups=mesh['tm'=4,'space'=2,'hyp'=4] {'tm'}, dimensions={0}, use_global_device_ids=true | all-gather | bytes 81920 | tf_op jit(solution)/shard_map/all_gather | solution.py:26
  152.2 13.1 %all-gather.3 = f32[16384]{0:T(1024)S(1)} all-gather(f32[4096]{0:T(1024)S(1)} %get-tuple-element.529), channel_id=5, replica_groups=mesh['tm'=4,'space'=2,'hyp'=4] {'tm'}, dimensions={0}, use_global_device_ids=true | all-gather | bytes 81920 | tf_op jit(solution)/shard_map/all_gather | solution.py:26
  166.7 43.2 %while.117 = (s32[]{:T(128)}, f32[4096]{0:T(1024)S(1)}, f32[4096]{0:T(1024)S(1)}, f32[1,4096]{1,0:T(1,128)S(1)}, f32[4096]{0:T(1024)S(1)}, /*index=5*/f32[4096]{...) while((s32[]{:T(128)}, f32[4096]{0:T(1024)S(1)}, ...), condition=%wide.region_6.7_spmd.clone, body=%wide.region_5.6_spmd.clone.sunk | while | flops 86019 | bytes 606413 | solution.py:150
  166.7 0.9 constant_dynamic-slice_fusion.31
  169.4 0.9 constant_dynamic-slice_fusion.31
  182.9 0.9 constant_dynamic-slice_fusion.31
  193.7 0.9 constant_dynamic-slice_fusion.31
  204.5 0.9 constant_dynamic-slice_fusion.31
  209.9 13.5 %all-gather.4 = f32[16384]{0:T(1024)S(1)} all-gather(f32[4096]{0:T(1024)S(1)} %get-tuple-element.534), channel_id=6, replica_groups=mesh['tm'=4,'space'=2,'hyp'=4] {'tm'}, dimensions={0}, use_global_device_ids=true | all-gather | bytes 81920 | tf_op jit(solution)/shard_map/all_gather | solution.py:26
  223.5 13.3 %all-gather.6 = f32[16384]{0:T(1024)S(1)} all-gather(f32[4096]{0:T(1024)S(1)} %get-tuple-element.536), channel_id=8, replica_groups=mesh['tm'=4,'space'=2,'hyp'=4] {'tm'}, dimensions={0}, use_global_device_ids=true | all-gather | bytes 81920 | tf_op jit(solution)/shard_map/all_gather | solution.py:26
  236.8 13.1 %all-gather.7 = f32[16384]{0:T(1024)S(1)} all-gather(f32[4096]{0:T(1024)S(1)} %get-tuple-element.537), channel_id=9, replica_groups=mesh['tm'=4,'space'=2,'hyp'=4] {'tm'}, dimensions={0}, use_global_device_ids=true | all-gather | bytes 81920 | tf_op jit(solution)/shard_map/all_gather | solution.py:26
  250.0 13.1 %all-gather.11 = f32[4,1,4096]{2,1,0:T(1,128)S(1)} all-gather(f32[1,1,4096]{2,1,0:T(1,128)S(1)} %bitcast.144), channel_id=7, replica_groups=mesh['tm'=4,'space'=2,'hyp'=4] {'tm'}, dimensions={0}, use_global_device_ids=true | all-gather | bytes 81920 | tf_op jit(solution)/shard_map/all_gather | solution.py:26
  263.4 14.6 %while.118 = (s32[]{:T(128)}, f32[4096]{0:T(1024)S(1)}, f32[4096]{0:T(1024)S(1)}, f32[16,4096]{1,0:T(8,128)S(1)}, f32[16,4096]{1,0:T(8,128)S(1)}, /*index=5*/f32...) while((s32[]{:T(128)}, f32[4096]{0:T(1024)S(1)}, ...), condition=%wide.region_10.11_spmd.clone, body=%wide.region_9.10_spmd.clone.sunk | while | flops 32772 | bytes 311443 | solution.py:170
  278.0 13.4 %all-gather.8 = f32[16384]{0:T(1024)S(1)} all-gather(f32[4096]{0:T(1024)S(1)} %get-tuple-element.542), channel_id=10, replica_groups=mesh['tm'=4,'space'=2,'hyp'=4] {'tm'}, dimensions={0}, use_global_device_ids=true | all-gather | bytes 81920 | tf_op jit(solution)/shard_map/all_gather | solution.py:26
  291.4 13.1 %all-gather.9 = f32[16384]{0:T(1024)S(1)} all-gather(f32[4096]{0:T(1024)S(1)} %get-tuple-element.543), channel_id=11, replica_groups=mesh['tm'=4,'space'=2,'hyp'=4] {'tm'}, dimensions={0}, use_global_device_ids=true | all-gather | bytes 81920 | tf_op jit(solution)/shard_map/all_gather | solution.py:26
  306.9 41.7 %all-gather.15.cloned.1.call-done = f32[16,5,4096]{2,1,0:T(8,128)} async-done(((f32[1,5,4096]{2,1,0:T(8,128)}), f32[16,5,4096]{2,1,0:T(8,128)}) %all-gather.15.cloned.1.call-update) | async-done | bytes 1310736 | tf_op jit(solution)/shard_map/all_gather | solution.py:196
  348.6 1.7 reduce_sum.49
  (382 shorter events, 61.7 us)
Async XLA Ops:
  7.2 341.4 %all-gather.15.cloned.1.call-start = ((), (), s32[]{:S(2)}) async-start(), calls=%async_computation | async-start | bytes 2228224 | tf_op jit(solution)/shard_map/all_gather | solution.py:196
  8.0 10.1 %collective-permute-start = (f32[64]{0:T(128)S(1)}, f32[64]{0:T(128)S(1)}, u32[]{:S(2)}, u32[]{:S(2)}) collective-permute-start(f32[64]{0:T(128)S(1)} %get-tuple-element.865), channel_id=1, source_target_pairs={{0,4},{1,5},{2,6},{3,7},{8,12},{9,13},{10,14},{11,15},{16,20},{17,... | collective-permute-start | bytes 776 | tf_op jit(solution)/shard_map/ppermute | solution.py:14
  11.4 6.7 %collective-permute-start.1 = (f32[64]{0:T(128)S(1)}, f32[64]{0:T(128)S(1)}, u32[]{:S(2)}, u32[]{:S(2)}) collective-permute-start(f32[64]{0:T(128)S(1)} %get-tuple-element.864), channel_id=1, source_target_pairs={{4,0},{5,1},{6,2},{7,3},{12,8},{13,9},{14,10},{15,11},{20,16},{21,... | collective-permute-start | bytes 776 | tf_op jit(solution)/shard_map/ppermute | solution.py:17
  18.2 90.7 %copy-start.3 = (s32[4,4096]{1,0:T(4,128)S(1)}, s32[4,4096]{1,0:T(4,128)}, u32[]{:S(2)}) copy-start(s32[4,4096]{1,0:T(4,128)} %param.26) | copy-start | bytes 196612
  18.2 90.7 %copy-start.4 = (f32[4,4096]{1,0:T(4,128)S(1)}, f32[4,4096]{1,0:T(4,128)}, u32[]{:S(2)}) copy-start(f32[4,4096]{1,0:T(4,128)} %param.25) | copy-start | bytes 196612
  18.3 90.8 %copy-start.5 = (f32[4096]{0:T(1024)S(1)}, f32[4096]{0:T(1024)}, u32[]{:S(2)}) copy-start(f32[4096]{0:T(1024)} %param.24) | copy-start | bytes 49156
  18.3 90.8 %copy-start.6 = (f32[4096]{0:T(1024)S(1)}, f32[4096]{0:T(1024)}, u32[]{:S(2)}) copy-start(f32[4096]{0:T(1024)} %param.22) | copy-start | bytes 49156
  18.3 90.8 %copy-start.7 = (f32[4096]{0:T(1024)S(1)}, f32[4096]{0:T(1024)}, u32[]{:S(2)}) copy-start(f32[4096]{0:T(1024)} %param.23) | copy-start | bytes 49156
  18.3 91.9 %copy-start = (f32[16,4096]{1,0:T(8,128)S(1)}, f32[16,4096]{1,0:T(8,128)}, u32[]{:S(2)}) copy-start(f32[16,4096]{1,0:T(8,128)} %param.29) | copy-start | bytes 786436
  18.3 91.9 %copy-start.1 = (f32[16,4096]{1,0:T(8,128)S(1)}, f32[16,4096]{1,0:T(8,128)}, u32[]{:S(2)}) copy-start(f32[16,4096]{1,0:T(8,128)} %param.27) | copy-start | bytes 786436
  18.3 91.9 %copy-start.2 = (f32[16,4096]{1,0:T(8,128)S(1)}, f32[16,4096]{1,0:T(8,128)}, u32[]{:S(2)}) copy-start(f32[16,4096]{1,0:T(8,128)} %param.28) | copy-start | bytes 786436
Sparse Core Ops, SparseCore 0:
  306.4 42.1 all-gather.14
